TPU v7x, 32 devices: a whole 2x2x4 slice. The times are simulated.
32 devices in a mesh: expert: 2 (over y), hidden: 16 (over z, x, core).
Axes of the slice: x: 2, y: 2, z: 4, core: 2. Of those that a mesh axis runs over, the one named last changes fastest.
Arguments:
- tokens: bfloat16 [192, 3072], P('expert', 'hidden'), may hold values from -6 to 6
- cotangent: bfloat16 [192, 3072], P('expert', 'hidden'), may hold values from -6 to 6
- w_gate: bfloat16 [2, 3072, 16384], P('expert', None, 'hidden'), may hold values from -0.15625 to 0.15625
- w_up: bfloat16 [2, 3072, 16384], P('expert', None, 'hidden'), may hold values from -0.15625 to 0.15625
- w_down: bfloat16 [2, 16384, 3072], P('expert', 'hidden'), may hold values from -0.046875 to 0.046875
- slot_token: int32 [2, 192], P(None, 'expert'), may hold values from 0 to 95, as said below
- slot_weight: float32 [2, 192], P(None, 'expert'), may hold values from 0.2 to 1
- keep_mask: int32 [2, 192, 16384], P('expert', None, 'hidden'), may hold values 0 or 1
Outputs:
- grad_tokens: bfloat16 [192, 3072], P('expert', 'hidden')
Inputs may be any that keep to these rules, and one draw needn't show every extreme that they name: `slot_token`: slots s of block g = s // 96 of every expert hold tokens of group g (token rows g * 96 to (g + 1) * 96 - 1); within one expert and one block the 96 entries are distinct; every slot is filled.
All inputs are finite; a program needn't handle non-finite values. No bound on the sum of `keep_mask` on one device may be relied on, other than what follows from the above.
Results may differ from a plain program's by a relative error of at most 0.012.
Values may be sent and summed in bfloat16 or wider, within the bound.
No kernel may reach another device: no remote copies, remote signals or barrier semaphores. Data moves between devices by JAX's collectives and lax.ppermute only.
A program may use at most 64 MiB of HBM per device.

v0:
```python
import jax
import jax.numpy as jnp
from jax import lax
from jax.sharding import PartitionSpec as P

keep_rate = 0.9


def gelu_tanh(values):
    return jax.nn.gelu(values, approximate=True)


def fold_slots(slot_values, one_hot):
    high_part = slot_values.astype(jnp.bfloat16)
    low_part = (slot_values - high_part.astype(jnp.float32)).astype(jnp.bfloat16)
    return jnp.dot(high_part, one_hot, preferred_element_type=jnp.float32) + jnp.dot(
        low_part, one_hot, preferred_element_type=jnp.float32
    )


def body(tokens, cotangent, w_gate, w_up, w_down, slot_token, slot_weight, keep_mask):
    gate_mat = w_gate[0]
    up_mat = w_up[0]
    down_mat = w_down[0]
    model_width = gate_mat.shape[0]
    expert_count = lax.axis_size("expert")
    expert_total = slot_token.shape[0]
    per_source = slot_token.shape[1]
    slot_count = expert_count * per_source
    group_tokens = tokens.shape[0]
    slot_list = slot_token.reshape(-1)
    weight_column = slot_weight.reshape(-1, 1)
    inv_keep = 1.0 / keep_rate
    chosen = tokens[slot_list].reshape(expert_total, per_source, -1)
    scaled = (weight_column * cotangent[slot_list].astype(jnp.float32)).astype(jnp.bfloat16)
    sent_cot = scaled.reshape(expert_total, per_source, -1)
    recv_inputs, recv_cot = (
        lax.all_to_all(chosen, "expert", split_axis=0, concat_axis=0, tiled=True),
        lax.all_to_all(sent_cot, "expert", split_axis=0, concat_axis=0, tiled=True),
    )
    slot_inputs = recv_inputs.reshape(slot_count, -1)
    slot_cot = recv_cot.reshape(slot_count, -1)
    part_inputs = lax.all_gather(slot_inputs, "hidden", axis=1, tiled=True)
    part_cot = lax.all_gather(slot_cot, "hidden", axis=1, tiled=True)
    gate_rows = gate_mat
    up_rows = up_mat
    gate_pre = jnp.dot(part_inputs, gate_rows, preferred_element_type=jnp.float32)
    up_pre = jnp.dot(part_inputs, up_rows, preferred_element_type=jnp.float32)
    grad_hidden = lax.dot_general(
        part_cot, down_mat, (((1,), (1,)), ((), ())), preferred_element_type=jnp.float32
    )
    activated, pullback = jax.vjp(gelu_tanh, gate_pre)
    grad_pre = grad_hidden * keep_mask[0].astype(jnp.float32) * inv_keep
    grad_up = (grad_pre * activated).astype(jnp.bfloat16)
    grad_gate = pullback(grad_pre * up_pre)[0].astype(jnp.bfloat16)
    one_hot = (slot_list[:, None] == jnp.arange(group_tokens, dtype=jnp.int32)[None, :]).astype(
        jnp.bfloat16
    )
    local_width = model_width // lax.axis_size("hidden")
    gate_rows = gate_mat
    up_rows = up_mat
    reduced = lax.psum_scatter(
        lax.dot_general(
            gate_rows, grad_gate, (((1,), (1,)), ((), ())), preferred_element_type=jnp.float32
        )
        + lax.dot_general(
            up_rows, grad_up, (((1,), (1,)), ((), ())), preferred_element_type=jnp.float32
        ),
        "hidden",
        scatter_dimension=0,
        tiled=True,
    )
    returned = lax.all_to_all(
        reduced.reshape(local_width, expert_count, per_source),
        "expert",
        split_axis=1,
        concat_axis=1,
        tiled=True,
    )
    token_sum = fold_slots(returned.reshape(local_width, -1), one_hot)
    return token_sum.T.astype(jnp.bfloat16)


def solution(mesh):
    in_specs = (
        P("expert", "hidden"),
        P("expert", "hidden"),
        P("expert", None, "hidden"),
        P("expert", None, "hidden"),
        P("expert", "hidden", None),
        P(None, "expert"),
        P(None, "expert"),
        P("expert", None, "hidden"),
    )
    out_specs = P("expert", "hidden")
    return jax.shard_map(body, mesh=mesh, in_specs=in_specs, out_specs=out_specs, check_vma=False)
```

profile of v0, /device:TPU:0, one launch (start us, length us, event | category | flops | bytes accessed | tf_op | source)
XLA Modules:
  0.0 205.2 jit_solution(17161815436193137995)
XLA Ops:
  6.5 0.0 copy-start
  6.5 0.0 all-gather.5.cloned.1.call-start
  6.5 0.8 reshape.59
  7.3 0.0 copy-done
  7.3 1.0 gather_fusion.1
  8.4 8.3 %all_to_all.15 = bf16[2,96,192]{2,1,0:T(8,128)(2,1)S(1)} all-to-all(bf16[2,96,192]{2,1,0:T(8,128)(2,1)S(1)} %bitcast.53), channel_id=1, replica_groups=mesh['expert'=2,'hidden'=16] {'expert'}, dimensions={0} | all-to-all | bytes 147456 | tf_op jit(solution)/shard_map/all_to_all | solution.py:38
  16.7 0.7 copy.12
  17.4 0.0 all-gather.5.cloned.1.call-update
  17.4 0.0 all-gather.3.cloned.1.call-start
  17.5 1.7 gather_fusion
  19.2 0.8 fusion.48
  19.9 6.7 %all_to_all.16 = bf16[2,96,192]{2,1,0:T(8,128)(2,1)S(1)} all-to-all(bf16[2,96,192]{2,1,0:T(8,128)(2,1)S(1)} %fusion.48), channel_id=1, replica_groups=mesh['expert'=2,'hidden'=16] {'expert'}, dimensions={0} | all-to-all | bytes 147456 | tf_op jit(solution)/shard_map/all_to_all | solution.py:39
  26.6 0.7 copy.11
  27.3 0.0 all-gather.3.cloned.1.call-update
  27.4 0.0 reduce-scatter.4.cloned.1.call-start
  27.4 30.1 %all-gather.5.cloned.1.call-done = bf16[192,3072]{0,1:T(8,128)(2,1)} async-done(((bf16[192,192]{0,1:T(8,128)(2,1)}), bf16[192,3072]{0,1:T(8,128)(2,1)}) %all-gather.5.cloned.1.call-update) | async-done | bytes 1179664 | tf_op jit(solution)/shard_map/all_gather | solution.py:43
  57.6 4.7 %fusion.2 = f32[192,1024]{1,0:T(8,128)S(1)} fusion(bf16[192,3072]{0,1:T(8,128)(2,1)} %all-gather.5.cloned.1.call-done, bf16[1,3072,1024]{2,1,0:T(8,128)(2,1)} %param.10), kind=kOutput, calls=%fused_computation.4 | convolution fusion | flops 1207959552 | bytes 8257536 | tf_op jit(solution)/shard_map/dot_general | solution.py:47
  62.3 0.0 copy-start.1
  62.3 36.2 %all-gather.3.cloned.1.call-done = bf16[192,3072]{0,1:T(8,128)(2,1)} async-done(((bf16[192,192]{0,1:T(8,128)(2,1)}), bf16[192,3072]{0,1:T(8,128)(2,1)}) %all-gather.3.cloned.1.call-update) | async-done | bytes 1179664 | tf_op jit(solution)/shard_map/all_gather | solution.py:44
  98.4 5.6 %fusion.22 = f32[192,1024]{1,0:T(8,128)S(1)} fusion(bf16[192,3072]{0,1:T(8,128)(2,1)} %all-gather.3.cloned.1.call-done, bf16[1,1024,3072]{2,1,0:T(8,128)(2,1)} %param.12, s32[1,192,1024]{2,1,0:T(8,128)} %param.15), kind=kOutput, calls=%fused_computation.16 | convolution fusion | flops 1208549376 | bytes 9043968 | tf_op jit(solution)/shard_map/dot_general | solution.py:49
  104.1 9.9 %fusion = f32[192,3072]{1,0:T(8,128)} fusion(bf16[1,3072,1024]{2,1,0:T(8,128)(2,1)} %param.10, f32[192,1024]{1,0:T(8,128)S(1)} %fusion.2, f32[192,1024]{1,0:T(8,128)S(1)} %fusion.22, bf16[192,3072]{0,1:T(8,128)(2,1)S(1)} %copy-done.1, bf16[1,3072,1024]{2,1,0:T(8,128)(2,1)} %param.11), kind=kOutput, calls=%fused_computation.2 | convolution fusion | flops 2420047872 | bytes 17694720 | tf_op jit(solution)/shard_map/dot_general | solution.py:63
  114.0 5.9 %fusion.13 = f32[3072,192]{0,1:T(8,128)S(1)} fusion(f32[192,3072]{1,0:T(8,128)} %fusion, bf16[1,3072,1024]{2,1,0:T(8,128)(2,1)} %param.11, f32[192,1024]{1,0:T(8,128)S(1)} %fusion.22, f32[192,1024]{1,0:T(8,128)} %copy-done.2), kind=kOutput, calls=%fused_computation.13 | convolution fusion | flops 1210515456 | bytes 12582912 | tf_op jit(solution)/shard_map/dot_general | solution.py:66
  120.0 0.0 copy-start.3
  120.0 2.3 %copy.13 = f32[3072,192]{1,0:T(8,128)} copy(f32[3072,192]{0,1:T(8,128)S(1)} %fusion.13) | data formatting | bytes 4718592
  122.3 0.0 reduce-scatter.4.cloned.1.call-update
  122.3 65.3 %reduce-scatter.4.cloned.1.call-done = f32[192,192]{1,0:T(8,128)} async-done(((f32[3072,192]{1,0:T(8,128)}), f32[192,192]{1,0:T(8,128)}) %reduce-scatter.4.cloned.1.call-update) | async-done | bytes 147472
  187.5 1.7 copy.14
  189.3 3.4 %all-to-all-start.2 = ((f32[192,2,96]{0,2,1:T(8,128)}), f32[192,2,96]{0,2,1:T(8,128)S(1)}, u32[]{:S(2)}, u32[]{:S(2)}) async-start(f32[192,2,96]{0,2,1:T(8,128)} %bitcast.10), calls=%async_computation.2 | async-start | bytes 393216 | tf_op jit(solution)/shard_map/all_to_all | solution.py:73
  192.7 0.1 eq.15
  192.8 4.7 %all-to-all-done.2 = f32[192,2,96]{0,2,1:T(8,128)S(1)} async-done(((f32[192,2,96]{0,2,1:T(8,128)}), f32[192,2,96]{0,2,1:T(8,128)S(1)}, u32[]{:S(2)}, u32[]{:S(2)}) %all-to-all-start.2) | async-done | bytes 147488 | tf_op jit(solution)/shard_map/all_to_all | solution.py:73
  197.5 0.3 fusion.50
  197.8 0.9 fusion.25
  (7 shorter events, 0.0 us)
Async XLA Ops:
  6.5 0.8 copy-start
  6.5 51.0 %all-gather.5.cloned.1.call-start = ((), (), s32[]{:S(2)}) async-start(), calls=%async_computation.5 | async-start | bytes 1671168 | tf_op jit(solution)/shard_map/all_gather | solution.py:43
  17.4 81.0 %all-gather.3.cloned.1.call-start = ((), (), s32[]{:S(2)}) async-start(), calls=%async_computation.4 | async-start | bytes 1671168 | tf_op jit(solution)/shard_map/all_gather | solution.py:44
  27.4 160.2 %reduce-scatter.4.cloned.1.call-start = ((), (), s32[]{:S(2)}) async-start(), calls=%async_computation.6 | async-start | bytes 3342336
  62.3 41.9 %copy-start.2 = (f32[192,1024]{1,0:T(8,128)}, f32[192,1024]{1,0:T(8,128)S(1)}, u32[]{:S(2)}) copy-start(f32[192,1024]{1,0:T(8,128)S(1)} %fusion.2) | copy-start | bytes 2359300
  62.3 41.9 %copy-start.1 = (bf16[192,3072]{0,1:T(8,128)(2,1)S(1)}, bf16[192,3072]{0,1:T(8,128)(2,1)}, u32[]{:S(2)}) copy-start(bf16[192,3072]{0,1:T(8,128)(2,1)} %all-gather.5.cloned.1.call-done) | copy-start | bytes 3538948
  120.0 72.7 %copy-start.3 = (s32[2,96]{1,0:T(2,128)S(1)}, s32[2,96]{1,0:T(2,128)}, u32[]{:S(2)}) copy-start(s32[2,96]{1,0:T(2,128)} %param.13) | copy-start | bytes 2308
  189.3 8.2 %all-to-all-start.2 = ((f32[192,2,96]{0,2,1:T(8,128)}), f32[192,2,96]{0,2,1:T(8,128)S(1)}, u32[]{:S(2)}, u32[]{:S(2)}) async-start(f32[192,2,96]{0,2,1:T(8,128)} %bitcast.10), calls=%async_computation.2 | async-start | bytes 393216 | tf_op jit(solution)/shard_map/all_to_all | solution.py:73
Sparse Core Ops, SparseCore 0:
  17.6 39.9 all-gather.4
  59.8 38.5 all-gather.2
  122.4 65.0 reduce-scatter.3
where the time goes:
time: 206 us; the launch traced here: 205 us
  waiting for transfers between devices  136 us (66%)
  matrix products  27.3 us (13%)
  blocking collectives  15 us (7%)
  between operations  13.2 us (6%)
  local copies, waits for them, and re-layouts  9.05 us (4%)
  starting transfers between devices  3.52 us (2%)
    unnamed x4, waiting for transfers between devices  65.3 us
    all_gather x1, waiting for transfers between devices, body(): part_cot = lax.all_gather(slot_cot, 'hidden', axis=1, tiled=True)  36.2 us
    all_gather x1, waiting for transfers between devices, body(): part_inputs = lax.all_gather(slot_inputs, 'hidden', axis=1, tiled=True)  30.1 us
    dot_general x1, matrix products, body(): lax.dot_general(gate_rows, grad_gate, (((1,), (1,)), ((), ())), preferred...  9.91 us
    all_to_all x1, blocking collectives, body(): lax.all_to_all(chosen, 'expert', split_axis=0, concat_axis=0, tiled=True)  8.33 us
    all_to_all x1, blocking collectives, body(): lax.all_to_all(sent_cot, 'expert', split_axis=0, concat_axis=0, tiled=True)  6.65 us
    dot_general x1, matrix products, body(): lax.dot_general(up_rows, grad_up, (((1,), (1,)), ((), ())), preferred_ele...  5.93 us
    dot_general x1, matrix products, body(): lax.dot_general(part_cot, down_mat, (((1,), (1,)), ((), ())), preferred_e...  5.65 us
  transfers between devices with their start and end apart: 4, of which 4 were waited for; matrix products, arithmetic and copies ran while one was open for 4% of the time, Pallas kernels for 0%

commit v1 on v0

--- a/solution.py
+++ b/solution.py
@@ -2,6 +2,7 @@
 import jax.numpy as jnp
 from jax import lax
 from jax.sharding import PartitionSpec as P
+from jax.lax import all_gather
 
 keep_rate = 0.9
 
@@ -40,8 +41,9 @@
     )
     slot_inputs = recv_inputs.reshape(slot_count, -1)
     slot_cot = recv_cot.reshape(slot_count, -1)
-    part_inputs = lax.all_gather(slot_inputs, "hidden", axis=1, tiled=True)
-    part_cot = lax.all_gather(slot_cot, "hidden", axis=1, tiled=True)
+    step_out = jnp.concatenate([slot_inputs, slot_cot], axis=0)
+    o_now = all_gather(step_out, "hidden", axis=1, tiled=True)
+    part_inputs, part_cot = jnp.split(o_now, [slot_inputs.shape[0]], 0)
     gate_rows = gate_mat
     up_rows = up_mat
     gate_pre = jnp.dot(part_inputs, gate_rows, preferred_element_type=jnp.float32)

time: 206 us -> 184 us (0.89)
  waiting for transfers between devices: 136 us -> 119 us
  blocking collectives: 15 us -> 0 us
  starting transfers between devices: 3.52 us -> 11.1 us
    all_gather x2 -> x1, waiting for transfers between devices: 66.3 us -> 43.2 us  [body(): o_now = all_gather(step_out, 'hidden', axis=1, tiled=True)]
    all_to_all x2 -> x0, blocking collectives: 15 us -> none  [the longest x1 8.33 us: body(): lax.all_to_all(chosen, 'expert', split_axis=0, concat_axis=0, tiled=True)]
    all_to_all x0 -> x2, starting transfers between devices: none -> 7.57 us  [the longest x1 4.23 us: body(): lax.all_to_all(sent_cot, 'expert', split_axis=0, concat_axis=0, tiled=True)]
    all_to_all x0 -> x2, waiting for transfers between devices: none -> 6.16 us  [the longest x1 4.13 us: body(): lax.all_to_all(chosen, 'expert', split_axis=0, concat_axis=0, tiled=True)]
    unnamed x10 -> x12, local copies, waits for them, and re-layouts: 4.04 us -> 4.96 us
    unnamed x4 -> x3, waiting for transfers between devices: 65.3 us -> 65.2 us
  transfers between devices with their start and end apart: 4 -> 5, of which waited for: 4 -> 5; matrix products, arithmetic and copies ran while one was open for 4% -> 1% of each run, Pallas kernels for 0% -> 0%
where the time goes in v1:
time: 184 us; the launch traced here: 183 us
  waiting for transfers between devices  119 us (65%)
  matrix products  27.8 us (15%)
  between operations  13.5 us (7%)
  starting transfers between devices  11.1 us (6%)
  local copies, waits for them, and re-layouts  9.32 us (5%)
  other arithmetic  2.2 us (1%)
    unnamed x3, waiting for transfers between devices  65.2 us
    all_gather x1, waiting for transfers between devices, body(): o_now = all_gather(step_out, 'hidden', axis=1, tiled=True)  43.2 us
    dot_general x1, matrix products, body(): lax.dot_general(gate_rows, grad_gate, (((1,), (1,)), ((), ())), preferred...  10.4 us
    dot_general x1, matrix products, body(): lax.dot_general(up_rows, grad_up, (((1,), (1,)), ((), ())), preferred_ele...  5.98 us
    dot_general x1, matrix products, body(): lax.dot_general(part_cot, down_mat, (((1,), (1,)), ((), ())), preferred_e...  5.43 us
    unnamed x12, local copies, waits for them, and re-layouts  4.96 us
    dot_general x1, matrix products, body(): jnp.dot(part_inputs, gate_rows, preferred_element_type=jnp.float32)  4.81 us
    all_to_all x1, waiting for transfers between devices, body(): lax.all_to_all(reduced.reshape(local_width, expert_count, per_source), 'e...  4.72 us
  transfers between devices with their start and end apart: 5, of which 5 were waited for; matrix products, arithmetic and copies ran while one was open for 1% of the time, Pallas kernels for 0%

profile of v1, /device:TPU:0, one launch (start us, length us, event | category | flops | bytes accessed | tf_op | source)
XLA Modules:
  0.0 183.1 jit_solution(10434137969681644414)
XLA Ops:
  6.5 0.8 reshape.59
  7.3 0.0 copy-done
  7.3 1.0 gather_fusion.1
  8.4 1.4 fusion.61
  9.8 4.2 %all-to-all-start.1 = ((bf16[2,96,192]{2,1,0:T(8,128)(2,1)}), bf16[2,96,192]{2,1,0:T(8,128)(2,1)S(1)}, u32[]{:S(2)}, u32[]{:S(2)}) async-start(bf16[2,96,192]{2,1,0:T(8,128)(2,1)} %fusion.61), calls=%async_computation.1 | async-start | bytes 196608 | tf_op jit(solution)/shard_map/all_to_all | solution.py:40
  14.0 2.3 %gather_fusion = bf16[192,192]{1,0:T(8,128)(2,1)} fusion(bf16[96,192]{1,0:T(8,128)(2,1)} %param.8, s32[1024]{0:T(1024)S(1)} %pad_clamp_fusion), kind=kCustom, calls=%fused_computation | custom fusion | bytes 148224 | tf_op jit(solution)/shard_map/gather | solution.py:35
  16.3 2.0 %all-to-all-done.1 = bf16[2,96,192]{2,1,0:T(8,128)(2,1)S(1)} async-done(((bf16[2,96,192]{2,1,0:T(8,128)(2,1)}), bf16[2,96,192]{2,1,0:T(8,128)(2,1)S(1)}, u32[]{:S(2)}, u32[]{:S(2)}) %all-to-all-start.1) | async-done | bytes 73760 | tf_op jit(solution)/shard_map/all_to_all | solution.py:40
  18.3 3.3 %all-to-all-start = ((bf16[2,96,192]{2,1,0:T(8,128)(2,1)}), bf16[2,96,192]{2,1,0:T(8,128)(2,1)S(1)}, u32[]{:S(2)}, u32[]{:S(2)}) async-start(bf16[2,96,192]{2,1,0:T(8,128)(2,1)} %bitcast.1), calls=%async_computation | async-start | bytes 196608 | tf_op jit(solution)/shard_map/all_to_all | solution.py:39
  21.7 0.0 all-gather.2.cloned.1.call-start
  21.7 0.1 copy.12
  21.8 4.1 %all-to-all-done = bf16[2,96,192]{2,1,0:T(8,128)(2,1)S(1)} async-done(((bf16[2,96,192]{2,1,0:T(8,128)(2,1)}), bf16[2,96,192]{2,1,0:T(8,128)(2,1)S(1)}, u32[]{:S(2)}, u32[]{:S(2)}) %all-to-all-start) | async-done | bytes 73760 | tf_op jit(solution)/shard_map/all_to_all | solution.py:39
  26.0 0.1 copy.11
  26.1 0.7 pad_maximum_fusion
  26.8 0.0 all-gather.2.cloned.1.call-update
  26.8 0.0 copy-start.4
  26.9 0.0 reduce-scatter.4.cloned.1.call-start
  26.9 43.2 %all-gather.2.cloned.1.call-done = bf16[384,3072]{0,1:T(8,128)(2,1)} async-done(((bf16[384,192]{0,1:T(8,128)(2,1)}), bf16[384,3072]{0,1:T(8,128)(2,1)}) %all-gather.2.cloned.1.call-update) | async-done | bytes 2359312 | tf_op jit(solution)/shard_map/all_gather | solution.py:45
  70.1 4.8 %fusion.2 = f32[192,1024]{1,0:T(8,128)S(1)} fusion(bf16[1,3072,1024]{2,1,0:T(8,128)(2,1)} %param.10, bf16[384,3072]{0,1:T(8,128)(2,1)} %all-gather.2.cloned.1.call-done), kind=kOutput, calls=%fused_computation.4 | convolution fusion | flops 1207959552 | bytes 8650752 | tf_op jit(solution)/shard_map/dot_general | solution.py:49
  75.0 5.4 %fusion.29 = f32[192,1024]{1,0:T(8,128)S(1)} fusion(bf16[1,1024,3072]{2,1,0:T(8,128)(2,1)} %param.12, bf16[384,3072]{0,1:T(8,128)(2,1)S(1)} %copy-done.3, s32[1,192,1024]{2,1,0:T(8,128)S(1)} %copy-done.4), kind=kOutput, calls=%fused_computation.19 | convolution fusion | flops 1208549376 | bytes 9437184 | tf_op jit(solution)/shard_map/dot_general | solution.py:51
  80.4 0.9 copy-done.1
  81.3 10.4 %fusion = f32[192,3072]{1,0:T(8,128)} fusion(bf16[1,3072,1024]{2,1,0:T(8,128)(2,1)} %param.10, f32[192,1024]{1,0:T(8,128)S(1)} %fusion.2, f32[192,1024]{1,0:T(8,128)S(1)} %fusion.29, bf16[1,3072,1024]{2,1,0:T(8,128)(2,1)} %param.11, bf16[384,3072]{0,1:T(8,128)(2,1)} %all-gather.2.cloned.1.call-done), kind=kOutput, calls=%fused_computation.2 | convolution fusion | flops 2420047872 | bytes 18087936 | tf_op jit(solution)/shard_map/dot_general | solution.py:65
  91.7 6.0 %fusion.13 = f32[3072,192]{0,1:T(8,128)S(1)} fusion(f32[192,3072]{1,0:T(8,128)} %fusion, bf16[1,3072,1024]{2,1,0:T(8,128)(2,1)} %param.11, f32[192,1024]{1,0:T(8,128)} %copy-done.1, f32[192,1024]{1,0:T(8,128)S(1)} %fusion.2), kind=kOutput, calls=%fused_computation.13 | convolution fusion | flops 1210515456 | bytes 12582912 | tf_op jit(solution)/shard_map/dot_general | solution.py:68
  97.6 2.3 %copy.13 = f32[3072,192]{1,0:T(8,128)} copy(f32[3072,192]{0,1:T(8,128)S(1)} %fusion.13) | data formatting | bytes 4718592
  99.9 0.0 reduce-scatter.4.cloned.1.call-update
  100.0 65.1 %reduce-scatter.4.cloned.1.call-done = f32[192,192]{1,0:T(8,128)} async-done(((f32[3072,192]{1,0:T(8,128)}), f32[192,192]{1,0:T(8,128)}) %reduce-scatter.4.cloned.1.call-update) | async-done | bytes 147472
  165.1 1.7 copy.14
  166.8 3.4 %all-to-all-start.2 = ((f32[192,2,96]{0,2,1:T(8,128)}), f32[192,2,96]{0,2,1:T(8,128)S(1)}, u32[]{:S(2)}, u32[]{:S(2)}) async-start(f32[192,2,96]{0,2,1:T(8,128)} %bitcast.10), calls=%async_computation.2 | async-start | bytes 393216 | tf_op jit(solution)/shard_map/all_to_all | solution.py:75
  170.3 0.0 copy-done.2
  170.3 0.1 eq.15
  170.4 4.7 %all-to-all-done.2 = f32[192,2,96]{0,2,1:T(8,128)S(1)} async-done(((f32[192,2,96]{0,2,1:T(8,128)}), f32[192,2,96]{0,2,1:T(8,128)S(1)}, u32[]{:S(2)}, u32[]{:S(2)}) %all-to-all-start.2) | async-done | bytes 147488 | tf_op jit(solution)/shard_map/all_to_all | solution.py:75
  175.1 0.3 fusion.63
  175.4 0.9 fusion.34
  (9 shorter events, 0.0 us)
Async XLA Ops:
  6.5 0.8 copy-start
  9.8 8.6 %all-to-all-start.1 = ((bf16[2,96,192]{2,1,0:T(8,128)(2,1)}), bf16[2,96,192]{2,1,0:T(8,128)(2,1)S(1)}, u32[]{:S(2)}, u32[]{:S(2)}) async-start(bf16[2,96,192]{2,1,0:T(8,128)(2,1)} %fusion.61), calls=%async_computation.1 | async-start | bytes 196608 | tf_op jit(solution)/shard_map/all_to_all | solution.py:40
  18.3 7.6 %all-to-all-start = ((bf16[2,96,192]{2,1,0:T(8,128)(2,1)}), bf16[2,96,192]{2,1,0:T(8,128)(2,1)S(1)}, u32[]{:S(2)}, u32[]{:S(2)}) async-start(bf16[2,96,192]{2,1,0:T(8,128)(2,1)} %bitcast.1), calls=%async_computation | async-start | bytes 196608 | tf_op jit(solution)/shard_map/all_to_all | solution.py:39
  21.7 48.4 %all-gather.2.cloned.1.call-start = ((), (), s32[]{:S(2)}) async-start(), calls=%async_computation.4 | async-start | bytes 2506752 | tf_op jit(solution)/shard_map/all_gather | solution.py:45
  26.8 48.1 %copy-start.4 = (s32[1,192,1024]{2,1,0:T(8,128)S(1)}, s32[1,192,1024]{2,1,0:T(8,128)}, u32[]{:S(2)}) copy-start(s32[1,192,1024]{2,1,0:T(8,128)} %param.15) | copy-start | bytes 2359300
  26.9 138.3 %reduce-scatter.4.cloned.1.call-start = ((), (), s32[]{:S(2)}) async-start(), calls=%async_computation.5 | async-start | bytes 3342336
  70.1 4.8 %copy-start.3 = (bf16[384,3072]{0,1:T(8,128)(2,1)S(1)}, bf16[384,3072]{0,1:T(8,128)(2,1)}, u32[]{:S(2)}) copy-start(bf16[384,3072]{0,1:T(8,128)(2,1)} %all-gather.2.cloned.1.call-done) | copy-start | bytes 7077892
  80.4 0.9 copy-start.1
  99.9 70.3 %copy-start.2 = (s32[2,96]{1,0:T(2,128)S(1)}, s32[2,96]{1,0:T(2,128)}, u32[]{:S(2)}) copy-start(s32[2,96]{1,0:T(2,128)} %param.13) | copy-start | bytes 2308
  166.8 8.2 %all-to-all-start.2 = ((f32[192,2,96]{0,2,1:T(8,128)}), f32[192,2,96]{0,2,1:T(8,128)S(1)}, u32[]{:S(2)}, u32[]{:S(2)}) async-start(f32[192,2,96]{0,2,1:T(8,128)} %bitcast.10), calls=%async_computation.2 | async-start | bytes 393216 | tf_op jit(solution)/shard_map/all_to_all | solution.py:75
Sparse Core Ops, SparseCore 0:
  27.0 43.1 all-gather.1
  100.1 64.9 reduce-scatter.3
